TPU v7x, 512 devices: a whole 4x4x16 slice. The times are simulated.
512 devices in a mesh: pair: 32 (over z_lo, y), loop: 16 (over x, z_hi, core).
Axes of the slice: x: 4, y: 4, z: 16 (z_hi: 2, z_lo: 8; z = z_hi * 8 + z_lo), core: 2. Of those that a mesh axis runs over, the one named last changes fastest.
Arguments:
- amplitudes: float32 [8192, 8192], P('pair', 'loop'), may hold values from -6 to 6
- integrals: float32 [2048, 8192], P(None, 'loop'), may hold values from -0.0625 to 0.0625
- pair_partner: int32 [8192], P('pair'), may hold values from 0 to 8191, as said below
- virtual_swap: int32 [2048], P('loop'), may hold values from 0 to 2047, as said below
Outputs:
- ladder_sym: float32 [2048, 8192], P('loop', 'pair')
Inputs may be any that keep to these rules, and one draw needn't show every extreme that they name: pair_partner[pair_partner[p]] = p, and pair_partner[p] lies in the aligned block of 256 pairs that starts 8192 / 2 pairs further on, counted modulo 8192. virtual_swap[virtual_swap[k]] = k, virtual_swap[k] != k, and virtual_swap[k] lies in the same aligned block of 64 ab pairs as k.
All inputs are finite; a program needn't handle non-finite values.
Results may differ from a plain program's by a relative error of at most 0.000071.
Values sent between devices are 32-bit elements; how exact they have to be, the bound alone decides.
No kernel may reach another device: no remote copies, remote signals or barrier semaphores. Data moves between devices by JAX's collectives and lax.ppermute only.
A program may use at most 64 MiB of HBM per device.

v0:
```python
import jax
import jax.numpy as jnp
from jax import lax
from jax.sharding import PartitionSpec as P


def shifted(x, axis, by):
    count = lax.axis_size(axis)
    return lax.ppermute(x, axis, [(i, (i + by) % count) for i in range(count)])


def local(amplitudes, integrals, pair_partner, virtual_swap):
    loop_count = lax.axis_size("loop")
    pair_count = lax.axis_size("pair")
    ab_local = integrals.shape[0] // loop_count
    ij_local = amplitudes.shape[0]
    slab = lax.all_to_all(integrals, "loop", split_axis=0, concat_axis=1, tiled=True)
    ladder = lax.dot_general(
        slab,
        lax.all_gather(amplitudes, "loop", axis=1, tiled=True),
        (((1,), (1,)), ((), ())),
        precision=lax.Precision.HIGHEST,
        preferred_element_type=jnp.float32,
    )
    mirror = shifted(ladder, "pair", pair_count // 2)
    swap_local = virtual_swap - lax.axis_index("loop") * ab_local
    partner_local = pair_partner % ij_local
    mirror = jnp.take(jnp.take(mirror, swap_local, axis=0), partner_local, axis=1)
    return ladder + mirror


def solution(mesh):
    in_specs = (P("pair", "loop"), P(None, "loop"), P("pair"), P("loop"))
    out_specs = P("loop", "pair")
    return jax.shard_map(local, mesh=mesh, in_specs=in_specs, out_specs=out_specs, check_vma=False)
```

profile of v0, /device:TPU:1, one launch (start us, length us, event | category | flops | bytes accessed | tf_op | source)
XLA Modules:
  0.0 387.8 jit_solution(8886406078017381639)
XLA Ops:
  6.5 0.0 copy-start.1
  6.5 0.0 copy-start
  6.5 19.2 %all-to-all-start = ((f32[16,128,512]{2,1,0:T(8,128)}), f32[16,128,512]{2,1,0:T(8,128)}, u32[]{:S(2)}, u32[]{:S(2)}) async-start(f32[16,128,512]{2,1,0:T(8,128)} %bitcast.8), calls=%async_computation | async-start | bytes 8388608 | tf_op jit(solution)/shard_map/all_to_all | solution.py:17
  25.7 0.0 all-gather.2.cloned.1.call-start
  25.8 0.7 all-gather.2.cloned.1.call-update
  26.5 0.0 copy-done.1
  26.5 0.0 copy-done
  26.5 115.3 %all-to-all-done = f32[16,128,512]{2,1,0:T(8,128)} async-done(((f32[16,128,512]{2,1,0:T(8,128)}), f32[16,128,512]{2,1,0:T(8,128)}, u32[]{:S(2)}, u32[]{:S(2)}) %all-to-all-start) | async-done | bytes 4194336 | tf_op jit(solution)/shard_map/all_to_all | solution.py:17
  141.8 5.3 %copy.9 = f32[128,16,512]{0,2,1:T(8,128)} copy(f32[128,16,512]{2,0,1:T(8,128)} %bitcast.1) | data formatting | bytes 8388608 | tf_op jit(solution)/shard_map/all_to_all | solution.py:17
  147.1 166.5 %all-gather.2.cloned.1.call-done = f32[256,8192]{1,0:T(8,128)} async-done(((f32[256,512]{1,0:T(8,128)}), f32[256,8192]{1,0:T(8,128)}) %all-gather.2.cloned.1.call-update) | async-done | bytes 8388624 | tf_op jit(solution)/shard_map/all_gather | solution.py:20
  313.6 11.4 %fusion.1 = f32[128,256]{1,0:T(8,128)S(1)} fusion(f32[128,8192]{0,1:T(8,128)} %bitcast.7, f32[256,8192]{1,0:T(8,128)} %all-gather.2.cloned.1.call-done), kind=kOutput, calls=%fused_computation.14 | convolution fusion | flops 3221225472 | bytes 12713984 | tf_op jit(solution)/shard_map/dot_general | solution.py:18
  325.0 49.9 %collective-permute-start = (f32[128,256]{1,0:T(8,128)S(1)}, f32[128,256]{1,0:T(8,128)S(1)}, u32[]{:S(2)}, u32[]{:S(2)}) collective-permute-start(f32[128,256]{1,0:T(8,128)S(1)} %fusion.1), channel_id=1, source_target_pairs={{0,256},{16,272},{32,288},{48,304},{64,320},{80,336},{96,352},{112... | collective-permute-start | bytes 393224 | tf_op jit(solution)/shard_map/ppermute | solution.py:9
  374.9 3.5 collective-permute-done
  378.5 0.8 gather_fusion
  379.2 0.1 broadcast_select_fusion
  379.3 0.1 copy.10
  379.4 0.7 gather_fusion.1
  380.2 0.1 copy.11
  380.3 0.7 bitcast_add_fusion
  (4 shorter events, 0.0 us)
Async XLA Ops:
  6.5 19.9 %copy-start.1 = (s32[128]{0:T(128)S(1)}, s32[128]{0:T(128)}, u32[]{:S(2)}) copy-start(s32[128]{0:T(128)} %param.7) | copy-start | bytes 1540
  6.5 20.0 %copy-start = (s32[256]{0:T(256)S(1)}, s32[256]{0:T(256)}, u32[]{:S(2)}) copy-start(s32[256]{0:T(256)} %param.6) | copy-start | bytes 3076
  6.5 135.3 %all-to-all-start = ((f32[16,128,512]{2,1,0:T(8,128)}), f32[16,128,512]{2,1,0:T(8,128)}, u32[]{:S(2)}, u32[]{:S(2)}) async-start(f32[16,128,512]{2,1,0:T(8,128)} %bitcast.8), calls=%async_computation | async-start | bytes 8388608 | tf_op jit(solution)/shard_map/all_to_all | solution.py:17
  25.7 287.9 %all-gather.2.cloned.1.call-start = ((), (), s32[]{:S(2)}) async-start(), calls=%async_computation.1 | async-start | bytes 8912896 | tf_op jit(solution)/shard_map/all_gather | solution.py:20
  325.0 53.5 %collective-permute-start = (f32[128,256]{1,0:T(8,128)S(1)}, f32[128,256]{1,0:T(8,128)S(1)}, u32[]{:S(2)}, u32[]{:S(2)}) collective-permute-start(f32[128,256]{1,0:T(8,128)S(1)} %fusion.1), channel_id=1, source_target_pairs={{0,256},{16,272},{32,288},{48,304},{64,320},{80,336},{96,352},{112... | collective-permute-start | bytes 393224 | tf_op jit(solution)/shard_map/ppermute | solution.py:9
Sparse Core Ops, SparseCore 0:
  29.9 283.7 all-gather.1
where the time goes:
time: 388 us
  waiting for transfers between devices  286 us (74%)
  starting transfers between devices  69.1 us (18%)
  between operations  13.5 us (3%)
  matrix products  11.4 us (3%)
  local copies, waits for them, and re-layouts  6.99 us (2%)
    all_gather x1, waiting for transfers between devices, local(): lax.all_gather(amplitudes, 'loop', axis=1, tiled=True)  167 us
    all_to_all x1, waiting for transfers between devices, local(): lax.all_to_all(integrals, 'loop', split_axis=0, concat_axis=1, tiled=True)  115 us
    ppermute x1, starting transfers between devices, shifted(): return lax.ppermute(x, axis, [(i, (i + by) % count) for i in range(count)])  49.9 us
    all_to_all x1, starting transfers between devices, local(): lax.all_to_all(integrals, 'loop', split_axis=0, concat_axis=1, tiled=True)  19.2 us
    dot_general x1, matrix products, local(): lax.dot_general(slab, lax.all_gather(amplitudes, 'loop', axis=1, tiled=Tr...  11.4 us
  transfers between devices with their start and end apart: 3, of which 3 were waited for; matrix products, arithmetic and copies ran while one was open for 1% of the time, Pallas kernels for 0%

commit v1 on v0

--- a/solution.py
+++ b/solution.py
@@ -17,7 +17,9 @@
     slab = lax.all_to_all(integrals, "loop", split_axis=0, concat_axis=1, tiled=True)
     ladder = lax.dot_general(
         slab,
-        lax.all_gather(amplitudes, "loop", axis=1, tiled=True),
+        jnp.concatenate(
+            lax.all_to_all(jnp.stack([amplitudes] * lax.axis_size("loop")), "loop", 0, 0), axis=1
+        ),
         (((1,), (1,)), ((), ())),
         precision=lax.Precision.HIGHEST,
         preferred_element_type=jnp.float32,

time: 388 us -> 642 us (1.65)
  the two profiles are of different devices: /device:TPU:1 before, /device:TPU:102 now
where the time goes in v1:
time: 642 us
  waiting for transfers between devices  410 us (64%)
  blocking collectives  193 us (30%)
  starting transfers between devices  19.2 us (3%)
  matrix products  13.1 us (2%)
    all_to_all x1, waiting for transfers between devices, local(): lax.all_to_all(jnp.stack([amplitudes] * lax.axis_size('loop')), 'loop', 0...  401 us
    all_to_all x1, blocking collectives, local(): lax.all_to_all(integrals, 'loop', split_axis=0, concat_axis=1, tiled=True)  193 us
    all_to_all x1, starting transfers between devices, local(): lax.all_to_all(jnp.stack([amplitudes] * lax.axis_size('loop')), 'loop', 0...  17.3 us
    dot_general x1, matrix products, local(): lax.dot_general(slab, jnp.concatenate(lax.all_to_all(jnp.stack([amplitude...  13.1 us
  transfers between devices with their start and end apart: 2, of which 2 were waited for; matrix products, arithmetic and copies ran while one was open for 0% of the time, Pallas kernels for 0%

profile of v1, /device:TPU:102, one launch (start us, length us, event | category | flops | bytes accessed | tf_op | source)
XLA Modules:
  0.0 641.9 jit_solution(16525026066991950324)
XLA Ops:
  0.0 0.0 copy-start
  0.0 193.0 %all_to_all.21 = f32[16,128,512]{2,1,0:T(8,128)} all-to-all(f32[16,128,512]{2,1,0:T(8,128)} %bitcast.15), channel_id=1, replica_groups=mesh['pair'=32,'loop'=16] {'loop'}, dimensions={0} | all-to-all | bytes 8388608 | tf_op jit(solution)/shard_map/all_to_all | solution.py:17
  193.0 0.0 copy-done
  193.0 4.3 stack.2
  197.3 0.0 copy-start.2
  197.3 0.0 copy-start.1
  197.3 17.3 %all-to-all-start.1 = ((f32[16,256,512]{2,1,0:T(8,128)}), f32[16,256,512]{2,1,0:T(8,128)}, u32[]{:S(2)}, u32[]{:S(2)}) async-start(f32[16,256,512]{2,1,0:T(8,128)} %stack.2), calls=%async_computation.1 | async-start | bytes 16777216 | tf_op jit(solution)/shard_map/all_to_all | solution.py:21
  214.6 0.0 copy-done.2
  214.6 0.0 copy-done.1
  214.7 400.5 %all-to-all-done.1 = f32[16,256,512]{2,1,0:T(8,128)} async-done(((f32[16,256,512]{2,1,0:T(8,128)}), f32[16,256,512]{2,1,0:T(8,128)}, u32[]{:S(2)}, u32[]{:S(2)}) %all-to-all-start.1) | async-done | bytes 8388640 | tf_op jit(solution)/shard_map/all_to_all | solution.py:21
  615.2 13.1 %fusion.3 = f32[128,256]{1,0:T(8,128)S(1)} fusion(f32[16,256,512]{2,1,0:T(8,128)} %all-to-all-done.1, f32[16,128,512]{2,1,0:T(8,128)} %all_to_all.21), kind=kOutput, calls=%fused_computation.5 | convolution fusion | flops 3221225472 | bytes 12713984 | tf_op jit(solution)/shard_map/dot_general | solution.py:18
  628.3 1.9 collective-permute-start
  630.3 9.2 %collective-permute-done = f32[128,256]{1,0:T(8,128)S(1)} collective-permute-done((f32[128,256]{1,0:T(8,128)S(1)}, f32[128,256]{1,0:T(8,128)S(1)}, u32[]{:S(2)}, u32[]{:S(2)}) %collective-permute-start) | collective-permute-done | bytes 131104 | tf_op jit(solution)/shard_map/ppermute | solution.py:9
  639.5 0.8 gather_fusion
  640.2 0.1 broadcast_select_fusion
  640.3 0.1 copy.5
  640.4 0.7 gather_fusion.1
  641.1 0.1 copy.6
  641.2 0.7 bitcast_add_fusion
  (4 shorter events, 0.0 us)
Async XLA Ops:
  0.0 193.0 %copy-start = (f32[256,512]{1,0:T(8,128)S(1)}, f32[256,512]{1,0:T(8,128)}, u32[]{:S(2)}) copy-start(f32[256,512]{1,0:T(8,128)} %param.4) | copy-start | bytes 1572868
  197.3 17.3 %copy-start.2 = (s32[128]{0:T(128)S(1)}, s32[128]{0:T(128)}, u32[]{:S(2)}) copy-start(s32[128]{0:T(128)} %param.7) | copy-start | bytes 1540
  197.3 17.4 %copy-start.1 = (s32[256]{0:T(256)S(1)}, s32[256]{0:T(256)}, u32[]{:S(2)}) copy-start(s32[256]{0:T(256)} %param.6) | copy-start | bytes 3076
  197.3 417.9 %all-to-all-start.1 = ((f32[16,256,512]{2,1,0:T(8,128)}), f32[16,256,512]{2,1,0:T(8,128)}, u32[]{:S(2)}, u32[]{:S(2)}) async-start(f32[16,256,512]{2,1,0:T(8,128)} %stack.2), calls=%async_computation.1 | async-start | bytes 16777216 | tf_op jit(solution)/shard_map/all_to_all | solution.py:21
  628.3 11.2 %collective-permute-start = (f32[128,256]{1,0:T(8,128)S(1)}, f32[128,256]{1,0:T(8,128)S(1)}, u32[]{:S(2)}, u32[]{:S(2)}) collective-permute-start(f32[128,256]{1,0:T(8,128)S(1)} %fusion.3), channel_id=1, source_target_pairs={{0,256},{16,272},{32,288},{48,304},{64,320},{80,336},{96,352},{112... | collective-permute-start | bytes 393224 | tf_op jit(solution)/shard_map/ppermute | solution.py:9
